TPU v7x, 128 devices: a whole 4x4x4 slice. The times are simulated.
128 devices in a mesh: dp: 8 (over x, core), seq: 16 (over z, y).
Axes of the slice: x: 4, y: 4, z: 4, core: 2. Of those that a mesh axis runs over, the one named last changes fastest.
Arguments:
- queries: bfloat16 [16384, 4096], P(('dp', 'seq')), may hold values from -5 to 5
- key_states: bfloat16 [16384, 512], P(('dp', 'seq')), may hold values from -5 to 5
- value_states: bfloat16 [16384, 512], P(('dp', 'seq')), may hold values from -6 to 6
- grad_out: bfloat16 [16384, 4096], P(('dp', 'seq')), may hold values from -6 to 6
- doc_lengths: int32 [32], replicated, may hold values from 1 to 2048, 16384 in all
Outputs:
- grad_queries: bfloat16 [16384, 4096], P(('dp', 'seq'))
- grad_keys: bfloat16 [16384, 512], P(('dp', 'seq'))
- grad_values: bfloat16 [16384, 512], P(('dp', 'seq'))
Inputs may be any that keep to these rules, and one draw needn't show every extreme that they name: `doc_lengths`: 32 documents packed in order, lengths summing to 16384; one document has exactly 2048 tokens.
All inputs are finite; a program needn't handle non-finite values.
Results may differ from a plain program's by a relative error of at most 0.014.
Values may be sent and summed in bfloat16 or wider, within the bound.
No kernel may reach another device: no remote copies, remote signals or barrier semaphores. Data moves between devices by JAX's collectives and lax.ppermute only.
A program may use at most 256 MiB of HBM per device.

v0:
```python
import functools

import jax
import jax.numpy as jnp
from jax import lax
from jax.experimental import pallas as pl
from jax.experimental.pallas import tpu as pltpu
from jax.sharding import PartitionSpec as P

KVH = 4
HD = 128
BQ = 512
BK = 512
NEG = -1e30


def from_behind(value, axis, steps):
    count = lax.axis_size(axis)
    initial, last = (max(0, -steps), min(count, count - steps))
    return lax.ppermute(value, axis, [(source, source + steps) for source in range(initial, last)])


def expand_heads(states, repeat):
    rows = states.shape[0]
    grouped = states.reshape(rows, KVH, HD)
    return jnp.repeat(grouped, repeat, axis=1).reshape(rows, KVH * repeat * HD)


def dot_t(a, b):
    return lax.dot_general(a, b, (((1,), (1,)), ((), ())), preferred_element_type=jnp.float32)


def attend_kernel(bounds_ref, mixed_ref, kv_ref, kt_ref, lo_ref, dq_ref, dk_ref, dv_ref, dq_acc, m_scr, l_scr, dl_scr):
    group = mixed_ref.shape[0]
    heads = dq_ref.shape[1] // HD
    tiles = group // BQ
    rim_tiles = group // BK
    scale = HD ** (-0.5)
    dk_ref[...] = jnp.zeros(dk_ref.shape, jnp.float32)
    dv_ref[...] = jnp.zeros(dv_ref.shape, jnp.float32)

    for h in range(heads):
        qcol = h * HD
        gcol = heads * HD + h * HD

        def query_tile(t, carry, qcol=qcol, gcol=gcol):
            qs = pl.multiple_of(t * BQ, BQ)
            q_blk = mixed_ref[pl.ds(qs, BQ), qcol : qcol + HD]
            g_blk = mixed_ref[pl.ds(qs, BQ), gcol : gcol + HD]
            lo = lo_ref[:, pl.ds(qs, BQ)]
            kt_lo = bounds_ref[t]
            kt_mid = bounds_ref[tiles + t]
            kt_hi = rim_tiles + t

            def allowed_at(kt):
                k_pos = kt * BK + lax.broadcasted_iota(jnp.int32, (BK, BQ), 0)
                q_pos = group + qs + lax.broadcasted_iota(jnp.int32, (BK, BQ), 1)
                return (k_pos >= lo) & (k_pos <= q_pos)

            def sweep(step):
                def masked(kt, c):
                    step(kt, True)
                    return c

                def interior(kt, c):
                    step(kt, False)
                    return c

                lax.fori_loop(kt_lo, kt_mid, masked, 0)
                lax.fori_loop(kt_mid, kt_hi, interior, 0)
                step(kt_hi, True)

            def forward_step(kt, masked):
                row = pl.multiple_of(kt * BK, BK)
                s = dot_t(kv_ref[pl.ds(row, BK), 0:HD], q_blk) * scale
                if masked:
                    s = jnp.where(allowed_at(kt), s, NEG)
                dp = dot_t(kv_ref[pl.ds(row, BK), HD : 2 * HD], g_blk)
                m_old = m_scr[...]
                m_new = jnp.maximum(m_old, jnp.max(s, axis=0, keepdims=True))
                alpha = jnp.exp(m_old - m_new)
                p = jnp.exp(s - m_new)
                l_scr[...] = alpha * l_scr[...] + jnp.sum(p, axis=0, keepdims=True)
                dl_scr[...] = alpha * dl_scr[...] + jnp.sum(p * dp, axis=0, keepdims=True)
                m_scr[...] = m_new

            m_scr[...] = jnp.full(m_scr.shape, NEG, jnp.float32)
            l_scr[...] = jnp.zeros(l_scr.shape, jnp.float32)
            dl_scr[...] = jnp.zeros(dl_scr.shape, jnp.float32)
            sweep(forward_step)
            inv_l = 1.0 / l_scr[...]
            l_scr[...] = inv_l
            dl_scr[...] = dl_scr[...] * inv_l
            dq_acc[...] = jnp.zeros(dq_acc.shape, jnp.float32)

            def backward_step(kt, masked):
                row = pl.multiple_of(kt * BK, BK)
                s = dot_t(kv_ref[pl.ds(row, BK), 0:HD], q_blk) * scale
                prob = jnp.exp(s - m_scr[...]) * l_scr[...]
                if masked:
                    prob = jnp.where(allowed_at(kt), prob, 0.0)
                dp = dot_t(kv_ref[pl.ds(row, BK), HD : 2 * HD], g_blk)
                ds = (prob * (dp - dl_scr[...]) * scale).astype(jnp.bfloat16)
                dk_ref[pl.ds(row, BK), :] += jnp.dot(ds, q_blk, preferred_element_type=jnp.float32)
                dv_ref[pl.ds(row, BK), :] += jnp.dot(
                    prob.astype(jnp.bfloat16), g_blk, preferred_element_type=jnp.float32
                )
                dq_acc[...] += jnp.dot(
                    kt_ref[:, pl.ds(row, BK)], ds, preferred_element_type=jnp.float32
                )

            sweep(backward_step)
            dq_ref[pl.ds(qs, BQ), qcol : qcol + HD] = dq_acc[...].T.astype(dq_ref.dtype)
            return carry

        lax.fori_loop(0, tiles, query_tile, 0)


def attend(bounds, mixed, kv, kt, lo, heads, interpret=False):
    group = mixed.shape[0]
    vmem = pltpu.MemorySpace.VMEM
    return pl.pallas_call(
        attend_kernel,
        out_shape=(
            jax.ShapeDtypeStruct((group, heads * HD), jnp.bfloat16),
            jax.ShapeDtypeStruct((2 * group, HD), jnp.float32),
            jax.ShapeDtypeStruct((2 * group, HD), jnp.float32),
        ),
        in_specs=[pl.BlockSpec(memory_space=pltpu.SMEM)]
        + [pl.BlockSpec(memory_space=vmem) for _ in range(4)],
        out_specs=tuple(pl.BlockSpec(memory_space=vmem) for _ in range(3)),
        scratch_shapes=[
            pltpu.VMEM((HD, BQ), jnp.float32),
            pltpu.VMEM((1, BQ), jnp.float32),
            pltpu.VMEM((1, BQ), jnp.float32),
            pltpu.VMEM((1, BQ), jnp.float32),
        ],
        compiler_params=pltpu.CompilerParams(vmem_limit_bytes=48 * 1024 * 1024),
        interpret=interpret,
    )(bounds, mixed, kv, kt, lo)


def key_bounds(lo, group):
    tiles = group // BQ
    kt_lo = lo[::BQ] // BK
    kt_hi = group // BK + jnp.arange(tiles, dtype=jnp.int32)
    kt_mid = jnp.clip((lo[BQ - 1 :: BQ] + BK - 1) // BK, kt_lo, kt_hi)
    return jnp.concatenate([kt_lo, kt_mid]).astype(jnp.int32)


def doc_starts(doc_lengths, positions):
    ends = jnp.cumsum(doc_lengths)
    starts = ends - doc_lengths
    return jnp.max(jnp.where(starts[None, :] <= positions[:, None], starts[None, :], 0), axis=1)


def body(queries, key_states, value_states, grad_out, doc_lengths):
    seq_count = lax.axis_size("seq")
    repeat = max(1, seq_count // KVH)
    rows = queries.shape[0]
    packed = jnp.concatenate(
        [
            queries.reshape(rows, seq_count, -1),
            grad_out.reshape(rows, seq_count, -1),
            expand_heads(key_states, repeat).reshape(rows, seq_count, -1),
            expand_heads(value_states, repeat).reshape(rows, seq_count, -1),
        ],
        axis=2,
    ).reshape(rows, -1)
    mixed = lax.all_to_all(packed, "seq", split_axis=1, concat_axis=0, tiled=True)
    group = mixed.shape[0]
    heads = queries.shape[1] // (seq_count * HD)
    kcol = 2 * heads * HD
    rim = from_behind(mixed[:, kcol : kcol + 2 * HD], "dp", 1)
    kv = jnp.concatenate([rim, mixed[:, kcol : kcol + 2 * HD]], axis=0)
    keys_t = kv[:, :HD].T
    root = lax.axis_index("dp") * group
    positions = root + jnp.arange(group, dtype=jnp.int32)
    lo = (doc_starts(doc_lengths, positions) - root + group).astype(jnp.int32)
    dq, dk, dv = attend(key_bounds(lo, group), mixed, kv, keys_t, lo.reshape(1, group), heads)
    rim_grad = jnp.concatenate([dk[:group], dv[:group]], axis=1).astype(jnp.bfloat16)
    back = from_behind(rim_grad, "dp", -1).astype(jnp.float32)
    own = (jnp.concatenate([dk[group:], dv[group:]], axis=1) + back).astype(jnp.bfloat16)
    out_packed = jnp.concatenate([dq, own], axis=1)
    returned = lax.all_to_all(out_packed, "seq", split_axis=0, concat_axis=1, tiled=True)
    returned = returned.reshape(rows, seq_count, -1)
    qw = heads * HD
    grad_queries = returned[:, :, :qw].reshape(rows, seq_count * qw)

    def fold(part):
        total = jnp.sum(part.astype(jnp.float32).reshape(rows, KVH, repeat, HD), axis=2)
        return total.reshape(rows, KVH * HD).astype(jnp.bfloat16)

    grad_keys = fold(returned[:, :, qw : qw + HD])
    grad_values = fold(returned[:, :, qw + HD : qw + 2 * HD])
    return (grad_queries, grad_keys, grad_values)


def solution(mesh):
    return jax.shard_map(
        body,
        mesh=mesh,
        in_specs=(
            P(("dp", "seq"), None),
            P(("dp", "seq"), None),
            P(("dp", "seq"), None),
            P(("dp", "seq"), None),
            P(),
        ),
        out_specs=(P(("dp", "seq"), None), P(("dp", "seq"), None), P(("dp", "seq"), None)),
        check_vma=False,
    )
```

profile of v0, /device:TPU:3, one launch (start us, length us, event | category | flops | bytes accessed | tf_op | source)
XLA Modules:
  0.0 174.0 jit_solution(3327841300822393534)
XLA Ops:
  0.6 0.0 copy-start.1
  0.6 1.1 copy.59
  1.8 1.0 copy.60
  2.8 1.6 copy.47
  4.4 0.0 copy-done.1
  4.4 0.7 copy.48
  5.1 0.1 broadcast_in_dim.21
  5.2 0.1 broadcast_in_dim.20
  5.3 0.3 pad_maximum_fusion
  5.6 46.1 %all_to_all.32 = bf16[128,16,768]{0,2,1:T(8,128)(2,1)S(1)} all-to-all(bf16[128,16,768]{0,2,1:T(8,128)(2,1)S(1)} %pad_maximum_fusion), channel_id=1, replica_groups=mesh['dp'=8,'seq'=16] {'seq'}, dimensions={1} | all-to-all | bytes 6291456 | tf_op jit(solution)/shard_map/all_to_all | solution.py:170
  51.7 0.5 copy_bitcast_fusion
  52.1 0.0 copy-start.2
  52.1 1.1 slice.47
  53.2 5.1 %collective-permute-start = (bf16[2048,256]{0,1:T(8,128)(2,1)}, bf16[2048,256]{0,1:T(8,128)(2,1)}, u32[]{:S(2)}, u32[]{:S(2)}) collective-permute-start(bf16[2048,256]{0,1:T(8,128)(2,1)} %slice.47), channel_id=1, source_target_pairs={{0,16},{16,32},{32,48},{48,64},{64,80},{80,96},{96,112},{1,17},{17... | collective-permute-start | bytes 3145736 | tf_op jit(solution)/shard_map/ppermute | solution.py:20
  58.3 0.0 copy-done.2
  58.3 0.1 copy.46
  58.4 0.1 reduce-window.9
  58.4 0.1 reduce.2
  58.6 0.1 select_reduce_fusion
  58.7 0.1 slice.37
  58.8 0.1 slice.36
  58.9 0.1 pad_add_fusion.bounds_ref
  59.0 2.8 %copy.52.mixed_ref = bf16[2048,768]{1,0:T(8,128)(2,1)} copy(bf16[2048,768]{0,1:T(8,128)(2,1)S(1)} %copy_bitcast_fusion) | data formatting | bytes 6291456 | tf_op jit(solution)/shard_map/all_to_all | solution.py:170
  61.8 8.5 %collective-permute-done = bf16[2048,256]{0,1:T(8,128)(2,1)} collective-permute-done((bf16[2048,256]{0,1:T(8,128)(2,1)}, bf16[2048,256]{0,1:T(8,128)(2,1)}, u32[]{:S(2)}, u32[]{:S(2)}) %collective-permute-start) | collective-permute-done | bytes 1048608 | tf_op jit(solution)/shard_map/ppermute | solution.py:20
  70.3 1.7 %pad_maximum_fusion.1 = bf16[4096,256]{0,1:T(8,128)(2,1)S(1)} fusion(bf16[2048,256]{0,1:T(8,128)(2,1)} %slice.47, bf16[2048,256]{0,1:T(8,128)(2,1)} %collective-permute-done), kind=kLoop, calls=%fused_computation.3 | loop fusion | flops 4194304 | bytes 4194304 | tf_op jit(solution)/shard_map/concatenate | solution.py:175
  72.1 2.5 %copy.53.kv_ref = bf16[4096,256]{1,0:T(8,128)(2,1)} copy(bf16[4096,256]{0,1:T(8,128)(2,1)S(1)} %pad_maximum_fusion.1) | data formatting | bytes 4194304 | tf_op jit(solution)/shard_map/concatenate | solution.py:175
  74.6 1.3 fusion.2.kt_ref
  75.9 48.5 %shard_map.76 = (bf16[2048,256]{1,0:T(8,128)(2,1)S(1)}, f32[4096,128]{1,0:T(8,128)S(1)}, f32[4096,128]{1,0:T(8,128)}) custom-call(s32[8]{0:T(128)S(1)} %pad_add_fusion.bounds_ref, bf16[2048,768]{1,0:T(8,128)(2,1)} %copy.52.mixed_ref, bf16[4096,256]{1,0:T(8,128)(2,1)} %copy.53.kv_ref, bf16[128,4096]{1,0:T(8,128)(2,1)S(1)} %fusion.2.kt_ref, s32[1,2048]{1,0:T(1,128)S(1)} %bitcast.27), custom_call_target="tpu_custom_call" | custom-call | tf_op jit(solution)/shard_map/pallas_call | solution.py:122
  124.4 0.1 slice.69
  124.4 1.3 slice.68
  125.7 0.0 copy-start
  125.7 0.1 pad_maximum_fusion.3
  125.8 2.1 %collective-permute-start.1 = (bf16[2048,256]{1,0:T(8,128)(2,1)S(1)}, bf16[2048,256]{1,0:T(8,128)(2,1)S(1)}, u32[]{:S(2)}, u32[]{:S(2)}) collective-permute-start(bf16[2048,256]{1,0:T(8,128)(2,1)S(1)} %pad_maximum_fusion.3), channel_id=1, source_target_pairs={{16,0},{32,16},{48,32},{64,48},{80,64},{96,80},{112,96},{17,1},{33... | collective-permute-start | bytes 3145736 | tf_op jit(solution)/shard_map/ppermute | solution.py:20
  127.9 0.1 slice.40
  128.0 0.0 copy-done
  128.0 0.1 slice.41
  128.1 14.0 %collective-permute-done.1 = bf16[2048,256]{1,0:T(8,128)(2,1)S(1)} collective-permute-done((bf16[2048,256]{1,0:T(8,128)(2,1)S(1)}, bf16[2048,256]{1,0:T(8,128)(2,1)S(1)}, u32[]{:S(2)}, u32[]{:S(2)}) %collective-permute-start.1) | collective-permute-done | bytes 1048608 | tf_op jit(solution)/shard_map/ppermute | solution.py:20
  142.1 0.3 fusion
  142.4 0.2 pad_maximum_fusion.2
  142.6 28.3 %all_to_all.33 = bf16[16,128,512]{2,1,0:T(8,128)(2,1)S(1)} all-to-all(bf16[16,128,512]{2,1,0:T(8,128)(2,1)S(1)} %bitcast.30), channel_id=1, replica_groups=mesh['dp'=8,'seq'=16] {'seq'}, dimensions={0} | all-to-all | bytes 4194304 | tf_op jit(solution)/shard_map/all_to_all | solution.py:185
  170.9 0.1 bitcast_reduce_fusion
  171.0 0.1 slice_bitcast_fusion
  171.1 1.1 copy.62
  172.2 0.1 copy.56
  172.3 0.8 copy.58
  173.1 0.1 copy.55
  173.2 0.8 copy.57
  (4 shorter events, 0.0 us)
Async XLA Ops:
  0.6 3.8 %copy-start.1 = (bf16[128,4096]{1,0:T(8,128)(2,1)S(1)}, bf16[128,4096]{1,0:T(8,128)(2,1)}, u32[]{:S(2)}) copy-start(bf16[128,4096]{1,0:T(8,128)(2,1)} %param.8) | copy-start | bytes 3145732
  52.1 6.2 %copy-start.2 = (s32[32]{0:T(128)S(1)}, s32[32]{0:T(128)}, u32[]{:S(2)}) copy-start(s32[32]{0:T(128)} %param.9) | copy-start | bytes 388
  53.2 17.1 %collective-permute-start = (bf16[2048,256]{0,1:T(8,128)(2,1)}, bf16[2048,256]{0,1:T(8,128)(2,1)}, u32[]{:S(2)}, u32[]{:S(2)}) collective-permute-start(bf16[2048,256]{0,1:T(8,128)(2,1)} %slice.47), channel_id=1, source_target_pairs={{0,16},{16,32},{32,48},{48,64},{64,80},{80,96},{96,112},{1,17},{17... | collective-permute-start | bytes 3145736 | tf_op jit(solution)/shard_map/ppermute | solution.py:20
  125.7 2.3 %copy-start = (f32[4096,128]{1,0:T(8,128)S(1)}, f32[4096,128]{1,0:T(8,128)}, u32[]{:S(2)}) copy-start(f32[4096,128]{1,0:T(8,128)} %get-tuple-element.8) | copy-start | bytes 6291460
  125.8 16.2 %collective-permute-start.1 = (bf16[2048,256]{1,0:T(8,128)(2,1)S(1)}, bf16[2048,256]{1,0:T(8,128)(2,1)S(1)}, u32[]{:S(2)}, u32[]{:S(2)}) collective-permute-start(bf16[2048,256]{1,0:T(8,128)(2,1)S(1)} %pad_maximum_fusion.3), channel_id=1, source_target_pairs={{16,0},{32,16},{48,32},{64,48},{80,64},{96,80},{112,96},{17,1},{33... | collective-permute-start | bytes 3145736 | tf_op jit(solution)/shard_map/ppermute | solution.py:20
where the time goes:
time: 176 us; the launch traced here: 174 us
  blocking collectives  74.4 us (42%)
  Pallas kernels  48.5 us (28%)
  waiting for transfers between devices  22.5 us (13%)
  local copies, waits for them, and re-layouts  16.2 us (9%)
  starting transfers between devices  7.11 us (4%)
  other arithmetic  4.42 us (3%)
    pallas_call x1, Pallas kernels, attend(): pl.pallas_call(attend_kernel, out_shape=(jax.ShapeDtypeStruct((group, hea...  48.5 us
    all_to_all x1, blocking collectives, body(): lax.all_to_all(packed, 'seq', split_axis=1, concat_axis=0, tiled=True)  46.1 us
    all_to_all x1, blocking collectives, body(): lax.all_to_all(out_packed, 'seq', split_axis=0, concat_axis=1, tiled=True)  28.3 us
    ppermute x2, waiting for transfers between devices, from_behind(): lax.ppermute(value, axis, [(source, source + steps) for source in range(i...  22.5 us
    ppermute x2, starting transfers between devices, from_behind(): lax.ppermute(value, axis, [(source, source + steps) for source in range(i...  7.11 us
    unnamed x11, local copies, waits for them, and re-layouts  3.92 us
  transfers between devices with their start and end apart: 2, of which 2 were waited for; matrix products, arithmetic and copies ran while one was open for 2% of the time, Pallas kernels for 0%

commit v1 on v0

v1 whole, which is shorter than its diff:
```python
import jax
import jax.numpy as jnp
from jax import lax
from jax.experimental import pallas as pl
from jax.experimental.pallas import tpu as pltpu
from jax.sharding import PartitionSpec as P

KVH = 4
HD = 128
BQ = 512
BK = 512
NEG = -1e30


def from_behind(value, axis, steps):
    count = lax.axis_size(axis)
    initial, last = (max(0, -steps), min(count, count - steps))
    return lax.ppermute(value, axis, [(source, source + steps) for source in range(initial, last)])


def expand_heads(states, repeat):
    rows = states.shape[0]
    grouped = states.reshape(rows, KVH, HD)
    return jnp.repeat(grouped, repeat, axis=1).reshape(rows, KVH * repeat * HD)


def dot_t(a, b):
    return lax.dot_general(a, b, (((1,), (1,)), ((), ())), preferred_element_type=jnp.float32)


def attend_kernel(
    meta_ref, mixed_ref, rim_ref, dq_ref, rim_out, own_out,
    kv_scr, kt_scr, lo_scr, dk_acc, dv_acc, dq_acc, m_scr, l_scr, dl_scr,
):
    group = mixed_ref.shape[0]
    heads = dq_ref.shape[1] // HD
    tiles = group // BQ
    rim_tiles = group // BK
    docs = meta_ref.shape[0] - 1
    scale = HD ** (-0.5)
    kcol = 2 * heads * HD
    root = meta_ref[0]

    kv_scr[0:group, :] = rim_ref[...]
    kv_scr[group : 2 * group, :] = mixed_ref[:, kcol : kcol + 2 * HD]
    for c in range(2 * group // BK):
        kt_scr[:, c * BK : (c + 1) * BK] = (
            kv_scr[c * BK : (c + 1) * BK, 0:HD].astype(jnp.float32).T.astype(jnp.bfloat16)
        )
    dk_acc[...] = jnp.zeros(dk_acc.shape, jnp.float32)
    dv_acc[...] = jnp.zeros(dv_acc.shape, jnp.float32)

    positions = root + lax.broadcasted_iota(jnp.int32, (1, group), 1)

    def start_of(d, carry):
        begin, lo = carry
        lo = jnp.where(begin <= positions, begin, lo)
        return begin + meta_ref[d + 1], lo

    _, lo_vec = lax.fori_loop(0, docs, start_of, (jnp.int32(0), jnp.zeros((1, group), jnp.int32)))
    lo_scr[...] = lo_vec - root + group

    def doc_start(position):
        def step(d, carry):
            begin, found = carry
            found = jnp.where(begin <= position, begin, found)
            return begin + meta_ref[d + 1], found

        return lax.fori_loop(0, docs, step, (jnp.int32(0), jnp.int32(0)))[1] - root + group

    for h in range(heads):
        qcol = h * HD
        gcol = heads * HD + h * HD

        def query_tile(t, carry, qcol=qcol, gcol=gcol):
            qs = pl.multiple_of(t * BQ, BQ)
            q_blk = mixed_ref[pl.ds(qs, BQ), qcol : qcol + HD]
            g_blk = mixed_ref[pl.ds(qs, BQ), gcol : gcol + HD]
            lo = lo_scr[:, pl.ds(qs, BQ)]
            kt_hi = rim_tiles + t
            kt_lo = doc_start(root + qs) // BK
            kt_mid = jnp.minimum(jnp.maximum((doc_start(root + qs + BQ - 1) + BK - 1) // BK, kt_lo), kt_hi)

            def allowed_at(kt):
                k_pos = kt * BK + lax.broadcasted_iota(jnp.int32, (BK, BQ), 0)
                q_pos = group + qs + lax.broadcasted_iota(jnp.int32, (BK, BQ), 1)
                return (k_pos >= lo) & (k_pos <= q_pos)

            def sweep(step):
                def masked(kt, c):
                    step(kt, True)
                    return c

                def interior(kt, c):
                    step(kt, False)
                    return c

                lax.fori_loop(kt_lo, kt_mid, masked, 0)
                lax.fori_loop(kt_mid, kt_hi, interior, 0)
                step(kt_hi, True)

            def forward_step(kt, masked):
                row = pl.multiple_of(kt * BK, BK)
                s = dot_t(kv_scr[pl.ds(row, BK), 0:HD], q_blk) * scale
                if masked:
                    s = jnp.where(allowed_at(kt), s, NEG)
                dp = dot_t(kv_scr[pl.ds(row, BK), HD : 2 * HD], g_blk)
                m_old = m_scr[...]
                m_new = jnp.maximum(m_old, jnp.max(s, axis=0, keepdims=True))
                alpha = jnp.exp(m_old - m_new)
                p = jnp.exp(s - m_new)
                l_scr[...] = alpha * l_scr[...] + jnp.sum(p, axis=0, keepdims=True)
                dl_scr[...] = alpha * dl_scr[...] + jnp.sum(p * dp, axis=0, keepdims=True)
                m_scr[...] = m_new

            m_scr[...] = jnp.full(m_scr.shape, NEG, jnp.float32)
            l_scr[...] = jnp.zeros(l_scr.shape, jnp.float32)
            dl_scr[...] = jnp.zeros(dl_scr.shape, jnp.float32)
            sweep(forward_step)
            inv_l = 1.0 / l_scr[...]
            l_scr[...] = inv_l
            dl_scr[...] = dl_scr[...] * inv_l
            dq_acc[...] = jnp.zeros(dq_acc.shape, jnp.float32)

            def backward_step(kt, masked):
                row = pl.multiple_of(kt * BK, BK)
                s = dot_t(kv_scr[pl.ds(row, BK), 0:HD], q_blk) * scale
                prob = jnp.exp(s - m_scr[...]) * l_scr[...]
                if masked:
                    prob = jnp.where(allowed_at(kt), prob, 0.0)
                dp = dot_t(kv_scr[pl.ds(row, BK), HD : 2 * HD], g_blk)
                ds = (prob * (dp - dl_scr[...]) * scale).astype(jnp.bfloat16)
                dk_acc[pl.ds(row, BK), :] += jnp.dot(ds, q_blk, preferred_element_type=jnp.float32)
                dv_acc[pl.ds(row, BK), :] += jnp.dot(
                    prob.astype(jnp.bfloat16), g_blk, preferred_element_type=jnp.float32
                )
                dq_acc[...] += jnp.dot(
                    kt_scr[:, pl.ds(row, BK)], ds, preferred_element_type=jnp.float32
                )

            sweep(backward_step)
            dq_ref[pl.ds(qs, BQ), qcol : qcol + HD] = dq_acc[...].T.astype(dq_ref.dtype)
            return carry

        lax.fori_loop(0, tiles, query_tile, 0)

    rim_out[:, 0:HD] = dk_acc[0:group, :].astype(rim_out.dtype)
    rim_out[:, HD : 2 * HD] = dv_acc[0:group, :].astype(rim_out.dtype)
    own_out[:, 0:HD] = dk_acc[group : 2 * group, :]
    own_out[:, HD : 2 * HD] = dv_acc[group : 2 * group, :]


def attend(meta, mixed, rim, heads, interpret=False):
    group = mixed.shape[0]
    vmem = pltpu.MemorySpace.VMEM
    return pl.pallas_call(
        attend_kernel,
        out_shape=(
            jax.ShapeDtypeStruct((group, heads * HD), jnp.bfloat16),
            jax.ShapeDtypeStruct((group, 2 * HD), jnp.bfloat16),
            jax.ShapeDtypeStruct((group, 2 * HD), jnp.float32),
        ),
        in_specs=[pl.BlockSpec(memory_space=pltpu.SMEM)]
        + [pl.BlockSpec(memory_space=vmem) for _ in range(2)],
        out_specs=tuple(pl.BlockSpec(memory_space=vmem) for _ in range(3)),
        scratch_shapes=[
            pltpu.VMEM((2 * group, 2 * HD), jnp.bfloat16),
            pltpu.VMEM((HD, 2 * group), jnp.bfloat16),
            pltpu.VMEM((1, group), jnp.int32),
            pltpu.VMEM((2 * group, HD), jnp.float32),
            pltpu.VMEM((2 * group, HD), jnp.float32),
            pltpu.VMEM((HD, BQ), jnp.float32),
            pltpu.VMEM((1, BQ), jnp.float32),
            pltpu.VMEM((1, BQ), jnp.float32),
            pltpu.VMEM((1, BQ), jnp.float32),
        ],
        compiler_params=pltpu.CompilerParams(vmem_limit_bytes=48 * 1024 * 1024),
        interpret=interpret,
    )(meta, mixed, rim)


def body(queries, key_states, value_states, grad_out, doc_lengths):
    seq_count = lax.axis_size("seq")
    repeat = max(1, seq_count // KVH)
    rows = queries.shape[0]

    def by_destination(x):
        return x.reshape(rows, seq_count, -1).transpose(1, 0, 2)

    packed = jnp.concatenate(
        [
            by_destination(queries),
            by_destination(grad_out),
            by_destination(expand_heads(key_states, repeat)),
            by_destination(expand_heads(value_states, repeat)),
        ],
        axis=2,
    )
    mixed = lax.all_to_all(packed, "seq", split_axis=0, concat_axis=0, tiled=True)
    mixed = mixed.reshape(seq_count * rows, -1)
    group = mixed.shape[0]
    heads = queries.shape[1] // (seq_count * HD)
    kcol = 2 * heads * HD
    rim = from_behind(mixed[:, kcol : kcol + 2 * HD], "dp", 1)
    root = lax.axis_index("dp") * group
    meta = jnp.concatenate([root.reshape(1), doc_lengths]).astype(jnp.int32)
    dq, rim_grad, own = attend(meta, mixed, rim, heads)
    back = from_behind(rim_grad, "dp", -1).astype(jnp.float32)
    own = (own + back).astype(jnp.bfloat16)
    out_packed = jnp.concatenate([dq, own], axis=1).reshape(seq_count, rows, -1)
    returned = lax.all_to_all(out_packed, "seq", split_axis=0, concat_axis=0, tiled=True)
    qw = heads * HD
    grad_queries = returned[:, :, :qw].transpose(1, 0, 2).reshape(rows, seq_count * qw)

    def fold(part):
        part = part.astype(jnp.float32).reshape(KVH, repeat, rows, HD)
        return jnp.sum(part, axis=1).transpose(1, 0, 2).reshape(rows, KVH * HD).astype(jnp.bfloat16)

    grad_keys = fold(returned[:, :, qw : qw + HD])
    grad_values = fold(returned[:, :, qw + HD : qw + 2 * HD])
    return (grad_queries, grad_keys, grad_values)


def solution(mesh):
    return jax.shard_map(
        body,
        mesh=mesh,
        in_specs=(
            P(("dp", "seq"), None),
            P(("dp", "seq"), None),
            P(("dp", "seq"), None),
            P(("dp", "seq"), None),
            P(),
        ),
        out_specs=(P(("dp", "seq"), None), P(("dp", "seq"), None), P(("dp", "seq"), None)),
        check_vma=False,
    )
```

time: 176 us -> 171 us (0.972)
  the two profiles are of different devices: /device:TPU:3 before, /device:TPU:2 now
where the time goes in v1:
time: 171 us; the launch traced here: 168 us
  blocking collectives  75.4 us (44%)
  Pallas kernels  42.9 us (25%)
  waiting for transfers between devices  26.4 us (15%)
  starting transfers between devices  13.4 us (8%)
  local copies, waits for them, and re-layouts  8.53 us (5%)
    all_to_all x1, blocking collectives, body(): lax.all_to_all(packed, 'seq', split_axis=0, concat_axis=0, tiled=True)  47.5 us
    pallas_call x1, Pallas kernels, attend(): pl.pallas_call(attend_kernel, out_shape=(jax.ShapeDtypeStruct((group, hea...  42.9 us
    all_to_all x1, blocking collectives, body(): lax.all_to_all(out_packed, 'seq', split_axis=0, concat_axis=0, tiled=True)  27.9 us
    ppermute x2, waiting for transfers between devices, from_behind(): lax.ppermute(value, axis, [(source, source + steps) for source in range(i...  26.4 us
    ppermute x2, starting transfers between devices, from_behind(): lax.ppermute(value, axis, [(source, source + steps) for source in range(i...  13.4 us
    unnamed x9, local copies, waits for them, and re-layouts  4.18 us
  transfers between devices with their start and end apart: 2, of which 2 were waited for; matrix products, arithmetic and copies ran while one was open for 0% of the time, Pallas kernels for 0%

profile of v1, /device:TPU:2, one launch (start us, length us, event | category | flops | bytes accessed | tf_op | source)
XLA Modules:
  0.0 168.3 jit_solution(5558175510192541869)
XLA Ops:
  0.6 0.0 copy-start
  0.6 0.9 copy-done
  1.6 0.9 copy_bitcast_fusion
  2.5 1.8 %bitcast_bitcast_fusion = (bf16[16,128,256]{2,1,0:T(8,128)(2,1)S(1)}, bf16[16,128,256]{2,1,0:T(8,128)(2,1)S(1)}) fusion(bf16[16,16,8,256]{3,2,1,0:T(8,128)(2,1)} %bitcast.47, bf16[16,16,8,256]{3,2,1,0:T(8,128)(2,1)} %bitcast.48), kind=kLoop, calls=%fused_computation.3 | loop fusion | bytes 4194304 | tf_op jit(solution)/shard_map/transpose | solution.py:188
  4.3 0.1 broadcast_in_dim.7
  4.4 0.1 broadcast_in_dim.6
  4.5 0.3 pad_maximum_fusion
  4.8 0.0 copy-start.2
  4.8 47.5 %all_to_all.10 = bf16[16,128,768]{2,1,0:T(8,128)(2,1)S(1)} all-to-all(bf16[16,128,768]{2,1,0:T(8,128)(2,1)S(1)} %pad_maximum_fusion), channel_id=1, replica_groups=mesh['dp'=8,'seq'=16] {'seq'}, dimensions={0} | all-to-all | bytes 6291456 | tf_op jit(solution)/shard_map/all_to_all | solution.py:199
  52.3 0.0 copy-start.1
  52.3 1.6 copy-done.1
  54.0 0.1 slice.16
  54.0 1.9 %collective-permute-start = (bf16[2048,256]{1,0:T(8,128)(2,1)S(1)}, bf16[2048,256]{1,0:T(8,128)(2,1)S(1)}, u32[]{:S(2)}, u32[]{:S(2)}) collective-permute-start(bf16[2048,256]{1,0:T(8,128)(2,1)S(1)} %slice.16), channel_id=1, source_target_pairs={{0,16},{16,32},{32,48},{48,64},{64,80},{80,96},{96,112},{1,17},{17... | collective-permute-start | bytes 3145736 | tf_op jit(solution)/shard_map/ppermute | solution.py:18
  56.0 0.0 copy-done.2
  56.0 0.1 pad_add_fusion.meta_ref
  56.1 14.1 %collective-permute-done.rim_ref = bf16[2048,256]{1,0:T(8,128)(2,1)S(1)} collective-permute-done((bf16[2048,256]{1,0:T(8,128)(2,1)S(1)}, bf16[2048,256]{1,0:T(8,128)(2,1)S(1)}, u32[]{:S(2)}, u32[]{:S(2)}) %collective-permute-start) | collective-permute-done | bytes 1048608 | tf_op jit(solution)/shard_map/ppermute | solution.py:18
  70.2 42.9 %shard_map.76 = (bf16[2048,256]{1,0:T(8,128)(2,1)S(1)}, bf16[2048,256]{1,0:T(8,128)(2,1)S(1)}, f32[2048,256]{1,0:T(8,128)S(1)}) custom-call(s32[33]{0:T(128)S(1)} %pad_add_fusion.meta_ref, bf16[2048,768]{1,0:T(8,128)(2,1)} %bitcast.42, bf16[2048,256]{1,0:T(8,128)(2,1)S(1)} %collective-permute-done.rim_ref), custom_call_target="tpu_custom_call" | custom-call | tf_op jit(solution)/shard_map/pallas_call | solution.py:156
  113.0 11.4 %collective-permute-start.1 = (bf16[2048,256]{1,0:T(8,128)(2,1)S(1)}, bf16[2048,256]{1,0:T(8,128)(2,1)S(1)}, u32[]{:S(2)}, u32[]{:S(2)}) collective-permute-start(bf16[2048,256]{1,0:T(8,128)(2,1)S(1)} %get-tuple-element.8), channel_id=1, source_target_pairs={{16,0},{32,16},{48,32},{64,48},{80,64},{96,80},{112,96},{17,1},{33... | collective-permute-start | bytes 3145736 | tf_op jit(solution)/shard_map/ppermute | solution.py:18
  124.5 12.3 %collective-permute-done.1 = bf16[2048,256]{1,0:T(8,128)(2,1)S(1)} collective-permute-done((bf16[2048,256]{1,0:T(8,128)(2,1)S(1)}, bf16[2048,256]{1,0:T(8,128)(2,1)S(1)}, u32[]{:S(2)}, u32[]{:S(2)}) %collective-permute-start.1) | collective-permute-done | bytes 1048608 | tf_op jit(solution)/shard_map/ppermute | solution.py:18
  136.8 0.3 add_convert_fusion
  137.0 0.2 pad_maximum_fusion.1
  137.2 27.9 %all_to_all.11 = bf16[16,128,512]{2,1,0:T(8,128)(2,1)S(1)} all-to-all(bf16[16,128,512]{2,1,0:T(8,128)(2,1)S(1)} %bitcast.43), channel_id=1, replica_groups=mesh['dp'=8,'seq'=16] {'seq'}, dimensions={0} | all-to-all | bytes 4194304 | tf_op jit(solution)/shard_map/all_to_all | solution.py:211
  165.1 0.1 slice_bitcast_fusion
  165.2 1.1 copy.31
  166.3 0.1 bitcast_reduce_fusion
  166.4 0.1 copy.24
  166.6 0.8 copy.26
  167.4 0.1 copy.23
  167.5 0.8 copy.25
  (1 shorter events, 0.0 us)
Async XLA Ops:
  0.6 0.9 copy-start
  4.8 51.1 %copy-start.2 = (s32[32]{0:T(128)S(1)}, s32[32]{0:T(128)}, u32[]{:S(2)}) copy-start(s32[32]{0:T(128)} %param.9) | copy-start | bytes 388
  52.3 1.7 copy-start.1
  54.0 16.1 %collective-permute-start = (bf16[2048,256]{1,0:T(8,128)(2,1)S(1)}, bf16[2048,256]{1,0:T(8,128)(2,1)S(1)}, u32[]{:S(2)}, u32[]{:S(2)}) collective-permute-start(bf16[2048,256]{1,0:T(8,128)(2,1)S(1)} %slice.16), channel_id=1, source_target_pairs={{0,16},{16,32},{32,48},{48,64},{64,80},{80,96},{96,112},{1,17},{17... | collective-permute-start | bytes 3145736 | tf_op jit(solution)/shard_map/ppermute | solution.py:18
  113.0 23.7 %collective-permute-start.1 = (bf16[2048,256]{1,0:T(8,128)(2,1)S(1)}, bf16[2048,256]{1,0:T(8,128)(2,1)S(1)}, u32[]{:S(2)}, u32[]{:S(2)}) collective-permute-start(bf16[2048,256]{1,0:T(8,128)(2,1)S(1)} %get-tuple-element.8), channel_id=1, source_target_pairs={{16,0},{32,16},{48,32},{64,48},{80,64},{96,80},{112,96},{17,1},{33... | collective-permute-start | bytes 3145736 | tf_op jit(solution)/shard_map/ppermute | solution.py:18

commit v2 on v1

--- a/solution.py
+++ b/solution.py
@@ -30,7 +30,7 @@
 
 def attend_kernel(
     meta_ref, mixed_ref, rim_ref, dq_ref, rim_out, own_out,
-    kv_scr, kt_scr, lo_scr, dk_acc, dv_acc, dq_acc, m_scr, l_scr, dl_scr,
+    kv_scr, kt_scr, lo_scr, dk_acc, dv_acc, dq_acc, m_scr, l_scr, dl_scr, s_scr, dp_scr,
 ):
     group = mixed_ref.shape[0]
     heads = dq_ref.shape[1] // HD
@@ -78,7 +78,7 @@
             g_blk = mixed_ref[pl.ds(qs, BQ), gcol : gcol + HD]
             lo = lo_scr[:, pl.ds(qs, BQ)]
             kt_hi = rim_tiles + t
-            kt_lo = doc_start(root + qs) // BK
+            kt_lo = jnp.maximum(doc_start(root + qs) // BK, t)
             kt_mid = jnp.minimum(jnp.maximum((doc_start(root + qs + BQ - 1) + BK - 1) // BK, kt_lo), kt_hi)
 
             def allowed_at(kt):
@@ -105,6 +105,8 @@
                 if masked:
                     s = jnp.where(allowed_at(kt), s, NEG)
                 dp = dot_t(kv_scr[pl.ds(row, BK), HD : 2 * HD], g_blk)
+                s_scr[kt - t] = s
+                dp_scr[kt - t] = dp
                 m_old = m_scr[...]
                 m_new = jnp.maximum(m_old, jnp.max(s, axis=0, keepdims=True))
                 alpha = jnp.exp(m_old - m_new)
@@ -124,11 +126,8 @@
 
             def backward_step(kt, masked):
                 row = pl.multiple_of(kt * BK, BK)
-                s = dot_t(kv_scr[pl.ds(row, BK), 0:HD], q_blk) * scale
-                prob = jnp.exp(s - m_scr[...]) * l_scr[...]
-                if masked:
-                    prob = jnp.where(allowed_at(kt), prob, 0.0)
-                dp = dot_t(kv_scr[pl.ds(row, BK), HD : 2 * HD], g_blk)
+                prob = jnp.exp(s_scr[kt - t] - m_scr[...]) * l_scr[...]
+                dp = dp_scr[kt - t]
                 ds = (prob * (dp - dl_scr[...]) * scale).astype(jnp.bfloat16)
                 dk_acc[pl.ds(row, BK), :] += jnp.dot(ds, q_blk, preferred_element_type=jnp.float32)
                 dv_acc[pl.ds(row, BK), :] += jnp.dot(
@@ -173,6 +172,8 @@
             pltpu.VMEM((1, BQ), jnp.float32),
             pltpu.VMEM((1, BQ), jnp.float32),
             pltpu.VMEM((1, BQ), jnp.float32),
+            pltpu.VMEM((group // BK + 1, BK, BQ), jnp.float32),
+            pltpu.VMEM((group // BK + 1, BK, BQ), jnp.float32),
         ],
         compiler_params=pltpu.CompilerParams(vmem_limit_bytes=48 * 1024 * 1024),
         interpret=interpret,

time: 171 us -> 162 us (0.947)
  the two profiles are of different devices: /device:TPU:2 before, /device:TPU:4 now
where the time goes in v2:
time: 162 us; the launch traced here: 159 us
  blocking collectives  75.7 us (47%)
  Pallas kernels  42.7 us (26%)
  waiting for transfers between devices  26.4 us (16%)
  local copies, waits for them, and re-layouts  8.53 us (5%)
  starting transfers between devices  3.84 us (2%)
    all_to_all x1, blocking collectives, body(): lax.all_to_all(packed, 'seq', split_axis=0, concat_axis=0, tiled=True)  47.5 us
    pallas_call x1, Pallas kernels, attend(): pl.pallas_call(attend_kernel, out_shape=(jax.ShapeDtypeStruct((group, hea...  42.7 us
    all_to_all x1, blocking collectives, body(): lax.all_to_all(out_packed, 'seq', split_axis=0, concat_axis=0, tiled=True)  28.2 us
    ppermute x2, waiting for transfers between devices, from_behind(): lax.ppermute(value, axis, [(source, source + steps) for source in range(i...  26.4 us
    unnamed x9, local copies, waits for them, and re-layouts  4.18 us
    ppermute x2, starting transfers between devices, from_behind(): lax.ppermute(value, axis, [(source, source + steps) for source in range(i...  3.84 us
  transfers between devices with their start and end apart: 2, of which 2 were waited for; matrix products, arithmetic and copies ran while one was open for 0% of the time, Pallas kernels for 0%

profile of v2, /device:TPU:4, one launch (start us, length us, event | category | flops | bytes accessed | tf_op | source)
XLA Modules:
  0.0 158.9 jit_solution(16193067182247413965)
XLA Ops:
  0.6 0.0 copy-start
  0.6 0.9 copy-done
  1.6 0.9 copy_bitcast_fusion
  2.5 1.8 %bitcast_bitcast_fusion = (bf16[16,128,256]{2,1,0:T(8,128)(2,1)S(1)}, bf16[16,128,256]{2,1,0:T(8,128)(2,1)S(1)}) fusion(bf16[16,16,8,256]{3,2,1,0:T(8,128)(2,1)} %bitcast.47, bf16[16,16,8,256]{3,2,1,0:T(8,128)(2,1)} %bitcast.48), kind=kLoop, calls=%fused_computation.3 | loop fusion | bytes 4194304 | tf_op jit(solution)/shard_map/transpose | solution.py:189
  4.3 0.1 broadcast_in_dim.7
  4.4 0.1 broadcast_in_dim.6
  4.5 0.3 pad_maximum_fusion
  4.8 0.0 copy-start.2
  4.8 47.5 %all_to_all.10 = bf16[16,128,768]{2,1,0:T(8,128)(2,1)S(1)} all-to-all(bf16[16,128,768]{2,1,0:T(8,128)(2,1)S(1)} %pad_maximum_fusion), channel_id=1, replica_groups=mesh['dp'=8,'seq'=16] {'seq'}, dimensions={0} | all-to-all | bytes 6291456 | tf_op jit(solution)/shard_map/all_to_all | solution.py:200
  52.3 0.0 copy-start.1
  52.3 1.6 %copy-done.1 = bf16[16,128,768]{2,1,0:T(8,128)(2,1)} copy-done((bf16[16,128,768]{2,1,0:T(8,128)(2,1)}, bf16[16,128,768]{2,1,0:T(8,128)(2,1)S(1)}, u32[]{:S(2)}) %copy-start.1) | copy-done | bytes 3145752
  54.0 0.1 slice.16
  54.0 1.9 %collective-permute-start = (bf16[2048,256]{1,0:T(8,128)(2,1)S(1)}, bf16[2048,256]{1,0:T(8,128)(2,1)S(1)}, u32[]{:S(2)}, u32[]{:S(2)}) collective-permute-start(bf16[2048,256]{1,0:T(8,128)(2,1)S(1)} %slice.16), channel_id=1, source_target_pairs={{0,16},{16,32},{32,48},{48,64},{64,80},{80,96},{96,112},{1,17},{17... | collective-permute-start | bytes 3145736 | tf_op jit(solution)/shard_map/ppermute | solution.py:18
  56.0 0.0 copy-done.2
  56.0 0.1 pad_add_fusion.meta_ref
  56.1 14.1 %collective-permute-done.rim_ref = bf16[2048,256]{1,0:T(8,128)(2,1)S(1)} collective-permute-done((bf16[2048,256]{1,0:T(8,128)(2,1)S(1)}, bf16[2048,256]{1,0:T(8,128)(2,1)S(1)}, u32[]{:S(2)}, u32[]{:S(2)}) %collective-permute-start) | collective-permute-done | bytes 1048608 | tf_op jit(solution)/shard_map/ppermute | solution.py:18
  70.2 42.7 %shard_map.76 = (bf16[2048,256]{1,0:T(8,128)(2,1)S(1)}, bf16[2048,256]{1,0:T(8,128)(2,1)S(1)}, f32[2048,256]{1,0:T(8,128)S(1)}) custom-call(s32[33]{0:T(128)S(1)} %pad_add_fusion.meta_ref, bf16[2048,768]{1,0:T(8,128)(2,1)} %bitcast.42, bf16[2048,256]{1,0:T(8,128)(2,1)S(1)} %collective-permute-done.rim_ref), custom_call_target="tpu_custom_call" | custom-call | tf_op jit(solution)/shard_map/pallas_call | solution.py:155
  112.9 1.9 %collective-permute-start.1 = (bf16[2048,256]{1,0:T(8,128)(2,1)S(1)}, bf16[2048,256]{1,0:T(8,128)(2,1)S(1)}, u32[]{:S(2)}, u32[]{:S(2)}) collective-permute-start(bf16[2048,256]{1,0:T(8,128)(2,1)S(1)} %get-tuple-element.8), channel_id=1, source_target_pairs={{16,0},{32,16},{48,32},{64,48},{80,64},{96,80},{112,96},{17,1},{33... | collective-permute-start | bytes 3145736 | tf_op jit(solution)/shard_map/ppermute | solution.py:18
  114.8 12.3 %collective-permute-done.1 = bf16[2048,256]{1,0:T(8,128)(2,1)S(1)} collective-permute-done((bf16[2048,256]{1,0:T(8,128)(2,1)S(1)}, bf16[2048,256]{1,0:T(8,128)(2,1)S(1)}, u32[]{:S(2)}, u32[]{:S(2)}) %collective-permute-start.1) | collective-permute-done | bytes 1048608 | tf_op jit(solution)/shard_map/ppermute | solution.py:18
  127.1 0.3 add_convert_fusion
  127.4 0.2 pad_maximum_fusion.1
  127.6 28.2 %all_to_all.11 = bf16[16,128,512]{2,1,0:T(8,128)(2,1)S(1)} all-to-all(bf16[16,128,512]{2,1,0:T(8,128)(2,1)S(1)} %bitcast.43), channel_id=1, replica_groups=mesh['dp'=8,'seq'=16] {'seq'}, dimensions={0} | all-to-all | bytes 4194304 | tf_op jit(solution)/shard_map/all_to_all | solution.py:212
  155.8 0.1 slice_bitcast_fusion
  155.9 1.1 copy.31
  156.9 0.1 bitcast_reduce_fusion
  157.1 0.1 copy.24
  157.2 0.8 copy.26
  158.0 0.1 copy.23
  158.1 0.8 copy.25
  (1 shorter events, 0.0 us)
Async XLA Ops:
  0.6 0.9 copy-start
  4.8 51.1 %copy-start.2 = (s32[32]{0:T(128)S(1)}, s32[32]{0:T(128)}, u32[]{:S(2)}) copy-start(s32[32]{0:T(128)} %param.9) | copy-start | bytes 388
  52.3 1.7 %copy-start.1 = (bf16[16,128,768]{2,1,0:T(8,128)(2,1)}, bf16[16,128,768]{2,1,0:T(8,128)(2,1)S(1)}, u32[]{:S(2)}) copy-start(bf16[16,128,768]{2,1,0:T(8,128)(2,1)S(1)} %all_to_all.10) | copy-start | bytes 9437188
  54.0 16.1 %collective-permute-start = (bf16[2048,256]{1,0:T(8,128)(2,1)S(1)}, bf16[2048,256]{1,0:T(8,128)(2,1)S(1)}, u32[]{:S(2)}, u32[]{:S(2)}) collective-permute-start(bf16[2048,256]{1,0:T(8,128)(2,1)S(1)} %slice.16), channel_id=1, source_target_pairs={{0,16},{16,32},{32,48},{48,64},{64,80},{80,96},{96,112},{1,17},{17... | collective-permute-start | bytes 3145736 | tf_op jit(solution)/shard_map/ppermute | solution.py:18
  112.9 14.2 %collective-permute-start.1 = (bf16[2048,256]{1,0:T(8,128)(2,1)S(1)}, bf16[2048,256]{1,0:T(8,128)(2,1)S(1)}, u32[]{:S(2)}, u32[]{:S(2)}) collective-permute-start(bf16[2048,256]{1,0:T(8,128)(2,1)S(1)} %get-tuple-element.8), channel_id=1, source_target_pairs={{16,0},{32,16},{48,32},{64,48},{80,64},{96,80},{112,96},{17,1},{33... | collective-permute-start | bytes 3145736 | tf_op jit(solution)/shard_map/ppermute | solution.py:18

commit v3 on v2

--- a/solution.py
+++ b/solution.py
@@ -1,3 +1,5 @@
+import functools
+
 import jax
 import jax.numpy as jnp
 from jax import lax
@@ -28,10 +30,19 @@
     return lax.dot_general(a, b, (((1,), (1,)), ((), ())), preferred_element_type=jnp.float32)
 
 
-def attend_kernel(
-    meta_ref, mixed_ref, rim_ref, dq_ref, rim_out, own_out,
-    kv_scr, kt_scr, lo_scr, dk_acc, dv_acc, dq_acc, m_scr, l_scr, dl_scr, s_scr, dp_scr,
-):
+def attend_kernel(phase, *refs):
+    if phase == "early":
+        meta_ref, mixed_ref, dq_ref, acc_out = refs[:4]
+        rim_ref = dq_in = acc_in = rim_out = None
+        scratch = refs[4:]
+    elif phase == "rim":
+        meta_ref, mixed_ref, rim_ref, dq_in, acc_in, dq_ref, acc_out, rim_out = refs[:8]
+        scratch = refs[8:]
+    else:
+        meta_ref, mixed_ref, dq_in, acc_in, dq_ref, acc_out = refs[:6]
+        rim_ref = rim_out = None
+        scratch = refs[6:]
+    kv_scr, kt_scr, lo_scr, dk_acc, dv_acc, dq_acc, m_scr, l_scr, dl_scr, s_scr, dp_scr = scratch
     group = mixed_ref.shape[0]
     heads = dq_ref.shape[1] // HD
     tiles = group // BQ
@@ -41,14 +52,24 @@
     kcol = 2 * heads * HD
     root = meta_ref[0]
 
-    kv_scr[0:group, :] = rim_ref[...]
     kv_scr[group : 2 * group, :] = mixed_ref[:, kcol : kcol + 2 * HD]
-    for c in range(2 * group // BK):
+    first_chunk = rim_tiles
+    if rim_ref is not None:
+        kv_scr[0:group, :] = rim_ref[...]
+        first_chunk = 0
+        dk_acc[0:group, :] = jnp.zeros((group, HD), jnp.float32)
+        dv_acc[0:group, :] = jnp.zeros((group, HD), jnp.float32)
+    for c in range(first_chunk, 2 * group // BK):
         kt_scr[:, c * BK : (c + 1) * BK] = (
             kv_scr[c * BK : (c + 1) * BK, 0:HD].astype(jnp.float32).T.astype(jnp.bfloat16)
         )
-    dk_acc[...] = jnp.zeros(dk_acc.shape, jnp.float32)
-    dv_acc[...] = jnp.zeros(dv_acc.shape, jnp.float32)
+    if acc_in is None:
+        dk_acc[group : 2 * group, :] = jnp.zeros((group, HD), jnp.float32)
+        dv_acc[group : 2 * group, :] = jnp.zeros((group, HD), jnp.float32)
+    else:
+        dk_acc[group : 2 * group, :] = acc_in[:, 0:HD]
+        dv_acc[group : 2 * group, :] = acc_in[:, HD : 2 * HD]
+        dq_ref[...] = dq_in[...]
 
     positions = root + lax.broadcasted_iota(jnp.int32, (1, group), 1)
 
@@ -67,6 +88,13 @@
             return begin + meta_ref[d + 1], found
 
         return lax.fori_loop(0, docs, step, (jnp.int32(0), jnp.int32(0)))[1] - root + group
+
+    def needs_rim(t, count):
+        return count + (doc_start(root + t * BQ) < group).astype(jnp.int32)
+
+    t_rim = lax.fori_loop(0, tiles, needs_rim, jnp.int32(0))
+    t_mid = t_rim + (tiles - t_rim + 1) // 2
+    t_first, t_last = {"early": (t_rim, t_mid), "rim": (0, t_rim), "late": (t_mid, tiles)}[phase]
 
     for h in range(heads):
         qcol = h * HD
@@ -141,27 +169,30 @@
             dq_ref[pl.ds(qs, BQ), qcol : qcol + HD] = dq_acc[...].T.astype(dq_ref.dtype)
             return carry
 
-        lax.fori_loop(0, tiles, query_tile, 0)
-
-    rim_out[:, 0:HD] = dk_acc[0:group, :].astype(rim_out.dtype)
-    rim_out[:, HD : 2 * HD] = dv_acc[0:group, :].astype(rim_out.dtype)
-    own_out[:, 0:HD] = dk_acc[group : 2 * group, :]
-    own_out[:, HD : 2 * HD] = dv_acc[group : 2 * group, :]
-
-
-def attend(meta, mixed, rim, heads, interpret=False):
+        lax.fori_loop(t_first, t_last, query_tile, 0)
+
+    if rim_out is not None:
+        rim_out[:, 0:HD] = dk_acc[0:group, :].astype(rim_out.dtype)
+        rim_out[:, HD : 2 * HD] = dv_acc[0:group, :].astype(rim_out.dtype)
+    acc_out[:, 0:HD] = dk_acc[group : 2 * group, :]
+    acc_out[:, HD : 2 * HD] = dv_acc[group : 2 * group, :]
+
+
+def attend(phase, meta, mixed, *rest, heads, interpret=False):
     group = mixed.shape[0]
     vmem = pltpu.MemorySpace.VMEM
+    out_shape = [
+        jax.ShapeDtypeStruct((group, heads * HD), jnp.bfloat16),
+        jax.ShapeDtypeStruct((group, 2 * HD), jnp.float32),
+    ]
+    if phase == "rim":
+        out_shape.append(jax.ShapeDtypeStruct((group, 2 * HD), jnp.bfloat16))
     return pl.pallas_call(
-        attend_kernel,
-        out_shape=(
-            jax.ShapeDtypeStruct((group, heads * HD), jnp.bfloat16),
-            jax.ShapeDtypeStruct((group, 2 * HD), jnp.bfloat16),
-            jax.ShapeDtypeStruct((group, 2 * HD), jnp.float32),
-        ),
+        functools.partial(attend_kernel, phase),
+        out_shape=tuple(out_shape),
         in_specs=[pl.BlockSpec(memory_space=pltpu.SMEM)]
-        + [pl.BlockSpec(memory_space=vmem) for _ in range(2)],
-        out_specs=tuple(pl.BlockSpec(memory_space=vmem) for _ in range(3)),
+        + [pl.BlockSpec(memory_space=vmem) for _ in range(1 + len(rest))],
+        out_specs=tuple(pl.BlockSpec(memory_space=vmem) for _ in out_shape),
         scratch_shapes=[
             pltpu.VMEM((2 * group, 2 * HD), jnp.bfloat16),
             pltpu.VMEM((HD, 2 * group), jnp.bfloat16),
@@ -177,7 +208,7 @@
         ],
         compiler_params=pltpu.CompilerParams(vmem_limit_bytes=48 * 1024 * 1024),
         interpret=interpret,
-    )(meta, mixed, rim)
+    )(meta, mixed, *rest)
 
 
 def body(queries, key_states, value_states, grad_out, doc_lengths):
@@ -205,8 +236,10 @@
     rim = from_behind(mixed[:, kcol : kcol + 2 * HD], "dp", 1)
     root = lax.axis_index("dp") * group
     meta = jnp.concatenate([root.reshape(1), doc_lengths]).astype(jnp.int32)
-    dq, rim_grad, own = attend(meta, mixed, rim, heads)
+    dq, acc = attend("early", meta, mixed, heads=heads)
+    dq, acc, rim_grad = attend("rim", meta, mixed, rim, dq, acc, heads=heads)
     back = from_behind(rim_grad, "dp", -1).astype(jnp.float32)
+    dq, own = attend("late", meta, mixed, dq, acc, heads=heads)
     own = (own + back).astype(jnp.bfloat16)
     out_packed = jnp.concatenate([dq, own], axis=1).reshape(seq_count, rows, -1)
     returned = lax.all_to_all(out_packed, "seq", split_axis=0, concat_axis=0, tiled=True)

time: 162 us -> 153 us (0.944)
  the two profiles are of different devices: /device:TPU:4 before, /device:TPU:5 now
where the time goes in v3:
time: 153 us; the launch traced here: 152 us
  blocking collectives  78 us (51%)
  Pallas kernels  43 us (28%)
  starting transfers between devices  19.2 us (13%)
  local copies, waits for them, and re-layouts  9.89 us (6%)
    all_to_all x1, blocking collectives, body(): lax.all_to_all(packed, 'seq', split_axis=0, concat_axis=0, tiled=True)  46.1 us
    pallas_call x3, Pallas kernels, attend(): pl.pallas_call(functools.partial(attend_kernel, phase), out_shape=tuple(o...  43 us
    all_to_all x1, blocking collectives, body(): lax.all_to_all(out_packed, 'seq', split_axis=0, concat_axis=0, tiled=True)  31.9 us
    ppermute x2, starting transfers between devices, from_behind(): lax.ppermute(value, axis, [(source, source + steps) for source in range(i...  19.2 us
    unnamed x11, local copies, waits for them, and re-layouts  5.55 us
  transfers between devices with their start and end apart: 2, of which 1 were waited for; matrix products, arithmetic and copies ran while one was open for 0% of the time, Pallas kernels for 19%

profile of v3, /device:TPU:5, one launch (start us, length us, event | category | flops | bytes accessed | tf_op | source)
XLA Modules:
  0.0 152.4 jit_solution(7419669350450839801)
XLA Ops:
  0.6 0.0 copy-start
  0.6 0.9 copy-done
  1.6 0.9 copy_bitcast_fusion
  2.5 1.8 %bitcast_bitcast_fusion = (bf16[16,128,256]{2,1,0:T(8,128)(2,1)S(1)}, bf16[16,128,256]{2,1,0:T(8,128)(2,1)S(1)}) fusion(bf16[16,16,8,256]{3,2,1,0:T(8,128)(2,1)} %bitcast.49, bf16[16,16,8,256]{3,2,1,0:T(8,128)(2,1)} %bitcast.50), kind=kLoop, calls=%fused_computation.3 | loop fusion | bytes 4194304 | tf_op jit(solution)/shard_map/transpose | solution.py:220
  4.3 0.1 broadcast_in_dim.7
  4.4 0.1 broadcast_in_dim.6
  4.5 0.3 pad_maximum_fusion
  4.8 0.0 copy-start.3
  4.8 46.1 %all_to_all.10 = bf16[16,128,768]{2,1,0:T(8,128)(2,1)S(1)} all-to-all(bf16[16,128,768]{2,1,0:T(8,128)(2,1)S(1)} %pad_maximum_fusion), channel_id=1, replica_groups=mesh['dp'=8,'seq'=16] {'seq'}, dimensions={0} | all-to-all | bytes 6291456 | tf_op jit(solution)/shard_map/all_to_all | solution.py:231
  50.9 0.0 copy-start.2
  50.9 1.7 %copy-done.2 = bf16[16,128,768]{2,1,0:T(8,128)(2,1)} copy-done((bf16[16,128,768]{2,1,0:T(8,128)(2,1)}, bf16[16,128,768]{2,1,0:T(8,128)(2,1)S(1)}, u32[]{:S(2)}) %copy-start.2) | copy-done | bytes 3145752
  52.6 0.1 slice.16
  52.7 4.8 %collective-permute-start = (bf16[2048,256]{1,0:T(8,128)(2,1)S(1)}, bf16[2048,256]{1,0:T(8,128)(2,1)S(1)}, u32[]{:S(2)}, u32[]{:S(2)}) collective-permute-start(bf16[2048,256]{1,0:T(8,128)(2,1)S(1)} %slice.16), channel_id=1, source_target_pairs={{0,16},{16,32},{32,48},{48,64},{64,80},{80,96},{96,112},{1,17},{17... | collective-permute-start | bytes 3145736 | tf_op jit(solution)/shard_map/ppermute | solution.py:20
  57.4 0.0 copy-done.3
  57.5 0.1 pad_add_fusion.refs_0_
  57.5 15.6 %shard_map.76 = (bf16[2048,256]{1,0:T(8,128)(2,1)S(1)}, f32[2048,256]{1,0:T(8,128)S(1)}) custom-call(s32[33]{0:T(128)S(1)} %pad_add_fusion.refs_0_, bf16[2048,768]{1,0:T(8,128)(2,1)} %bitcast.42), custom_call_target="tpu_custom_call" | custom-call | tf_op jit(solution)/shard_map/pallas_call | solution.py:190
  73.2 0.0 copy-start.1
  73.2 1.4 copy-done.1
  74.5 0.0 collective-permute-done.refs_2_
  74.5 14.6 %shard_map.77 = (bf16[2048,256]{1,0:T(8,128)(2,1)S(1)}, f32[2048,256]{1,0:T(8,128)}, bf16[2048,256]{1,0:T(8,128)(2,1)S(1)}) custom-call(s32[33]{0:T(128)S(1)} %pad_add_fusion.refs_0_, bf16[2048,768]{1,0:T(8,128)(2,1)} %bitcast.43, bf16[2048,256]{1,0:T(8,128)(2,1)S(1)} %collective-permute-done.refs_2_, bf16[2048,256]{1,0:T(8,128)(2,1)S(1)} %get-tuple-element.10.refs_3_, ...), custom_call_target="tpu_custom_call" | custom-call | tf_op jit(solution)/shard_map/pallas_call | solution.py:190
  89.1 14.4 %collective-permute-start.1 = (bf16[2048,256]{1,0:T(8,128)(2,1)S(1)}, bf16[2048,256]{1,0:T(8,128)(2,1)S(1)}, u32[]{:S(2)}, u32[]{:S(2)}) collective-permute-start(bf16[2048,256]{1,0:T(8,128)(2,1)S(1)} %get-tuple-element.16), channel_id=1, source_target_pairs={{16,0},{32,16},{48,32},{64,48},{80,64},{96,80},{112,96},{17,1},{33... | collective-permute-start | bytes 3145736 | tf_op jit(solution)/shard_map/ppermute | solution.py:20
  103.6 12.8 %shard_map.78 = (bf16[2048,256]{1,0:T(8,128)(2,1)S(1)}, f32[2048,256]{1,0:T(8,128)S(1)}) custom-call(s32[33]{0:T(128)S(1)} %pad_add_fusion.refs_0_, bf16[2048,768]{1,0:T(8,128)(2,1)} %bitcast.44, bf16[2048,256]{1,0:T(8,128)(2,1)S(1)} %get-tuple-element.12.refs_2_, f32[2048,256]{1,0:T(8,128)} %get-tuple-element.13.refs_3_), custom_call_target="tpu_custom_call" | custom-call | tf_op jit(solution)/shard_map/pallas_call | solution.py:190
  116.4 0.5 collective-permute-done.1
  116.8 0.3 add_convert_fusion
  117.2 0.2 pad_maximum_fusion.1
  117.3 31.9 %all_to_all.11 = bf16[16,128,512]{2,1,0:T(8,128)(2,1)S(1)} all-to-all(bf16[16,128,512]{2,1,0:T(8,128)(2,1)S(1)} %bitcast.45), channel_id=1, replica_groups=mesh['dp'=8,'seq'=16] {'seq'}, dimensions={0} | all-to-all | bytes 4194304 | tf_op jit(solution)/shard_map/all_to_all | solution.py:245
  149.3 0.1 slice_bitcast_fusion
  149.4 1.1 copy.31
  150.4 0.1 bitcast_reduce_fusion
  150.6 0.1 copy.24
  150.7 0.8 copy.26
  151.5 0.1 copy.23
  151.6 0.8 copy.25
  (1 shorter events, 0.0 us)
Async XLA Ops:
  0.6 0.9 copy-start
  4.8 52.6 %copy-start.3 = (s32[32]{0:T(128)S(1)}, s32[32]{0:T(128)}, u32[]{:S(2)}) copy-start(s32[32]{0:T(128)} %param.9) | copy-start | bytes 388
  50.9 1.7 %copy-start.2 = (bf16[16,128,768]{2,1,0:T(8,128)(2,1)}, bf16[16,128,768]{2,1,0:T(8,128)(2,1)S(1)}, u32[]{:S(2)}) copy-start(bf16[16,128,768]{2,1,0:T(8,128)(2,1)S(1)} %all_to_all.10) | copy-start | bytes 9437188
  52.7 21.9 %collective-permute-start = (bf16[2048,256]{1,0:T(8,128)(2,1)S(1)}, bf16[2048,256]{1,0:T(8,128)(2,1)S(1)}, u32[]{:S(2)}, u32[]{:S(2)}) collective-permute-start(bf16[2048,256]{1,0:T(8,128)(2,1)S(1)} %slice.16), channel_id=1, source_target_pairs={{0,16},{16,32},{32,48},{48,64},{64,80},{80,96},{96,112},{1,17},{17... | collective-permute-start | bytes 3145736 | tf_op jit(solution)/shard_map/ppermute | solution.py:20
  73.2 1.4 copy-start.1
  89.1 27.7 %collective-permute-start.1 = (bf16[2048,256]{1,0:T(8,128)(2,1)S(1)}, bf16[2048,256]{1,0:T(8,128)(2,1)S(1)}, u32[]{:S(2)}, u32[]{:S(2)}) collective-permute-start(bf16[2048,256]{1,0:T(8,128)(2,1)S(1)} %get-tuple-element.16), channel_id=1, source_target_pairs={{16,0},{32,16},{48,32},{64,48},{80,64},{96,80},{112,96},{17,1},{33... | collective-permute-start | bytes 3145736 | tf_op jit(solution)/shard_map/ppermute | solution.py:20
